TPU v7x, 512 devices: a whole 4x8x8 slice. The times are simulated.
512 devices in a mesh: seq: 64 (over z, y), head: 8 (over x, core).
Axes of the slice: x: 4, y: 8, z: 8, core: 2. Of those that a mesh axis runs over, the one named last changes fastest.
Arguments:
- queries: bfloat16 [2, 4096, 8192], P(None, 'seq', 'head'), may hold values from -10 to 10
- key_states: bfloat16 [2, 4096, 1024], P(None, ('seq', 'head')), may hold values from -10 to 10
- value_state_rows: bfloat16 [2, 4096, 1024], P(None, ('seq', 'head')), may hold values from -6 to 6
- grad_out: bfloat16 [2, 4096, 8192], P(None, 'seq', 'head'), may hold values from -6 to 6
- layouts: int32 [4, 128, 8], replicated, may hold values from 0 to 127, as said below
- plant_ids: int32 [128], replicated, may hold values from 0 to 3
Outputs:
- attended: bfloat16 [2, 4096, 8192], P(None, 'seq', 'head')
- query_grad: bfloat16 [2, 4096, 8192], P(None, 'seq', 'head')
- key_grad: bfloat16 [2, 4096, 1024], P(None, ('seq', 'head'))
- value_grad: bfloat16 [2, 4096, 1024], P(None, ('seq', 'head'))
Inputs may be any that keep to these rules, and one draw needn't show every extreme that they name: Entry 0 of layouts[p, q] is q and every entry is at most q. With owner(b) = b for b < 64 and 127 - b otherwise: if an entry b of layouts[p, q] has owner(b) = o other than owner(q) = d, then b = o when o < d and b = 127 - o when o > d.
All inputs are finite; a program needn't handle non-finite values.
Results may differ from a plain program's by a relative error of at most 0.011.
Values may be sent and summed in bfloat16 or wider, within the bound.
No kernel may reach another device: no remote copies, remote signals or barrier semaphores. Data moves between devices by JAX's collectives and lax.ppermute only.
A program may use at most 64 MiB of HBM per device.

v0:
```python
import jax
import jax.numpy as jnp
from jax import lax
from jax.sharding import PartitionSpec as P

HEAD_SIZE = 128
BLOCK_TOKENS_N = 64
KEY_LIST_SIZE = 8


def live_entries(listed_blocks):
    same_block = listed_blocks[:, None] == listed_blocks[None, :]
    ordinal = jnp.arange(listed_blocks.shape[0], dtype=jnp.int32)
    earlier = ordinal[None, :] < ordinal[:, None]
    return jnp.logical_not(jnp.any(same_block & earlier, axis=1))


def allowed_mask(listed_blocks, live_entry, qblock):
    offsets = jnp.arange(BLOCK_TOKENS_N, dtype=jnp.int32)
    causal = offsets[None, :] <= offsets[:, None]
    diagonal = listed_blocks == qblock
    allowed = live_entry[:, None, None] & (jnp.logical_not(diagonal)[:, None, None] | causal[None])
    return jnp.transpose(allowed, (1, 0, 2)).reshape(BLOCK_TOKENS_N, KEY_LIST_SIZE * BLOCK_TOKENS_N)


def attend_block(query_row_values, gradient_rows, keys_sel, values_sel, allowed, scaling):
    kv_heads = keys_sel.shape[2] // HEAD_SIZE
    head_groups = query_row_values.shape[1] // (kv_heads * HEAD_SIZE)
    query_head_rows = query_row_values.reshape(BLOCK_TOKENS_N, kv_heads, head_groups, HEAD_SIZE)
    gradient_heads = gradient_rows.reshape(BLOCK_TOKENS_N, kv_heads, head_groups, HEAD_SIZE)
    key_head_rows = keys_sel.reshape(KEY_LIST_SIZE * BLOCK_TOKENS_N, kv_heads, HEAD_SIZE)
    value_head_rows = values_sel.reshape(KEY_LIST_SIZE * BLOCK_TOKENS_N, kv_heads, HEAD_SIZE)
    scores = (
        jnp.einsum(
            "qhgd,khd->hgqk", query_head_rows, key_head_rows, preferred_element_type=jnp.float32
        )
        * scaling
    )
    scores = jnp.where(allowed[None, None], scores, -1e30)
    row_max = jnp.max(scores, axis=-1, keepdims=True)
    exponent = jnp.exp(scores - row_max)
    normed = exponent / jnp.sum(exponent, axis=-1, keepdims=True)
    weights = normed.astype(jnp.bfloat16)
    block_out = jnp.einsum(
        "hgqk,khd->qhgd", weights, value_head_rows, preferred_element_type=jnp.float32
    )
    block_out = block_out.astype(jnp.bfloat16).reshape(BLOCK_TOKENS_N, -1)
    grad_probs = jnp.einsum(
        "qhgd,khd->hgqk", gradient_heads, value_head_rows, preferred_element_type=jnp.float32
    )
    row_delta = jnp.sum(normed * grad_probs, axis=-1, keepdims=True)
    grad_scores = (normed * (grad_probs - row_delta)).astype(jnp.bfloat16)
    block_dq = (
        jnp.einsum("hgqk,khd->qhgd", grad_scores, key_head_rows, preferred_element_type=jnp.float32)
        * scaling
    )
    block_dq = block_dq.astype(jnp.bfloat16).reshape(BLOCK_TOKENS_N, -1)
    key_portion = (
        jnp.einsum(
            "hgqk,qhgd->khd", grad_scores, query_head_rows, preferred_element_type=jnp.float32
        )
        * scaling
    )
    value_portion = jnp.einsum(
        "hgqk,qhgd->khd", weights, gradient_heads, preferred_element_type=jnp.float32
    )
    key_portion = key_portion.reshape(KEY_LIST_SIZE, BLOCK_TOKENS_N, kv_heads * HEAD_SIZE)
    value_portion = value_portion.reshape(KEY_LIST_SIZE, BLOCK_TOKENS_N, kv_heads * HEAD_SIZE)
    return (block_out, block_dq, key_portion, value_portion)


def body(queries, key_states, value_state_rows, grad_out, layouts, plant_ids):
    scaling = HEAD_SIZE ** (-0.5)
    seq_count = lax.axis_size("seq")
    device = lax.axis_index("seq")
    count_of_blocks = layouts.shape[1]
    halfway = count_of_blocks // 2
    mine_keys, mine_values = (
        lax.all_to_all(key_states, "head", split_axis=2, concat_axis=1, tiled=True),
        lax.all_to_all(value_state_rows, "head", split_axis=2, concat_axis=1, tiled=True),
    )
    qblocks = jnp.stack([device, count_of_blocks - 1 - device])
    pick_block = jnp.arange(count_of_blocks, dtype=jnp.int32)[None, :] == qblocks[:, None]
    plant_of = jnp.sum(jnp.where(pick_block, plant_ids[None, :], 0), axis=1)
    pick_plant = jnp.arange(layouts.shape[0], dtype=jnp.int32)[None, :] == plant_of[:, None]
    picked = pick_plant[:, :, None, None] & pick_block[:, None, :, None]
    listed_all = jnp.sum(jnp.where(picked, layouts[None], 0), axis=(1, 2))
    owners = jnp.where(listed_all < halfway, listed_all, count_of_blocks - 1 - listed_all)
    upper_half = (listed_all >= halfway).astype(jnp.int32)
    slot_of = jnp.where(owners == device, seq_count + upper_half, owners)
    pool_keys, pool_values = (
        lax.all_gather(mine_keys, "seq", axis=0, tiled=True),
        lax.all_gather(mine_values, "seq", axis=0, tiled=True),
    )
    pool_index = 2 * owners + upper_half
    width = mine_keys.shape[2]
    key_buffer = jnp.zeros((seq_count + 2, BLOCK_TOKENS_N, width), jnp.float32)
    value_buffer = jnp.zeros((seq_count + 2, BLOCK_TOKENS_N, width), jnp.float32)
    slot_ids = jnp.arange(seq_count + 2, dtype=jnp.int32)
    outputs = []
    query_grads = []
    for which_half in range(2):
        listed_blocks = listed_all[which_half]
        live_entry = live_entries(listed_blocks)
        allowed = allowed_mask(listed_blocks, live_entry, qblocks[which_half])
        chosen_index = pool_index[which_half]
        block_out, block_dq, key_portion, value_portion = attend_block(
            queries[which_half],
            grad_out[which_half],
            pool_keys[chosen_index],
            pool_values[chosen_index],
            allowed,
            scaling,
        )
        outputs.append(block_out)
        query_grads.append(block_dq)
        routing = (
            (slot_ids[:, None] == slot_of[which_half][None, :]) & live_entry[None, :]
        ).astype(jnp.float32)
        key_buffer = key_buffer + jnp.einsum(
            "sj,jbf->sbf", routing, key_portion, precision=lax.Precision.HIGHEST
        )
        value_buffer = value_buffer + jnp.einsum(
            "sj,jbf->sbf", routing, value_portion, precision=lax.Precision.HIGHEST
        )
    back_keys, back_values = (
        lax.all_to_all(
            key_buffer[:seq_count].astype(jnp.bfloat16),
            "seq",
            split_axis=0,
            concat_axis=0,
            tiled=True,
        ).astype(jnp.float32),
        lax.all_to_all(
            value_buffer[:seq_count].astype(jnp.bfloat16),
            "seq",
            split_axis=0,
            concat_axis=0,
            tiled=True,
        ).astype(jnp.float32),
    )
    from_higher = (jnp.arange(seq_count, dtype=jnp.int32) > device).astype(jnp.float32)[
        :, None, None
    ]
    from_lower = 1.0 - from_higher
    lower_key = key_buffer[seq_count] + jnp.sum(back_keys * from_higher, axis=0)
    upper_key = key_buffer[seq_count + 1] + jnp.sum(back_keys * from_lower, axis=0)
    lower_value = value_buffer[seq_count] + jnp.sum(back_values * from_higher, axis=0)
    upper_value = value_buffer[seq_count + 1] + jnp.sum(back_values * from_lower, axis=0)
    key_total = jnp.stack([lower_key, upper_key]).astype(jnp.bfloat16)
    value_total = jnp.stack([lower_value, upper_value]).astype(jnp.bfloat16)
    key_grad, value_grad = (
        lax.all_to_all(key_total, "head", split_axis=1, concat_axis=2, tiled=True),
        lax.all_to_all(value_total, "head", split_axis=1, concat_axis=2, tiled=True),
    )
    return (jnp.stack(outputs), jnp.stack(query_grads), key_grad, value_grad)


def solution(mesh):
    in_specs = (
        P(None, "seq", "head"),
        P(None, ("seq", "head"), None),
        P(None, ("seq", "head"), None),
        P(None, "seq", "head"),
        P(),
        P(),
    )
    out_specs = (
        P(None, "seq", "head"),
        P(None, "seq", "head"),
        P(None, ("seq", "head"), None),
        P(None, ("seq", "head"), None),
    )
    return jax.shard_map(body, mesh=mesh, in_specs=in_specs, out_specs=out_specs, check_vma=False)
```

profile of v0, /device:TPU:1, one launch (start us, length us, event | category | flops | bytes accessed | tf_op | source)
XLA Modules:
  0.0 306.1 jit_solution(1030200950925951874)
XLA Ops:
  7.3 1.1 copy.63
  8.9 13.9 %all_to_all.82 = bf16[8,2,1024]{2,1,0:T(2,128)(2,1)S(1)} all-to-all(bf16[8,2,1024]{2,1,0:T(2,128)(2,1)S(1)} %reshape.429), channel_id=1, replica_groups=mesh['seq'=64,'head'=8] {'head'}, dimensions={0} | all-to-all | bytes 65536 | tf_op jit(solution)/shard_map/all_to_all | solution.py:79
  25.4 7.8 %all_to_all.83 = bf16[8,2,1024]{2,1,0:T(2,128)(2,1)S(1)} all-to-all(bf16[8,2,1024]{2,1,0:T(2,128)(2,1)S(1)} %reshape.427), channel_id=1, replica_groups=mesh['seq'=64,'head'=8] {'head'}, dimensions={0} | all-to-all | bytes 65536 | tf_op jit(solution)/shard_map/all_to_all | solution.py:80
  36.9 66.1 %all-gather.5.cloned.1.call-done = bf16[128,64,128]{2,1,0:T(8,128)(2,1)} async-done(((bf16[2,64,128]{2,1,0:T(8,128)(2,1)}), bf16[128,64,128]{2,1,0:T(8,128)(2,1)}) %all-gather.5.cloned.1.call-update) | async-done | bytes 2097168 | tf_op jit(solution)/shard_map/all_gather | solution.py:92
  103.0 2.2 gather_fusion.3
  105.9 81.0 %all-gather.3.cloned.1.call-done = bf16[128,64,128]{2,1,0:T(8,128)(2,1)} async-done(((bf16[2,64,128]{2,1,0:T(8,128)(2,1)}), bf16[128,64,128]{2,1,0:T(8,128)(2,1)}) %all-gather.3.cloned.1.call-update) | async-done | bytes 2097168 | tf_op jit(solution)/shard_map/all_gather | solution.py:93
  186.9 2.2 gather_fusion.2
  190.8 1.0 fusion.8
  191.9 2.2 gather_fusion.1
  194.8 2.2 gather_fusion
  198.8 1.2 fusion.32
  200.0 1.3 convolution_add_fusion.1
  201.3 1.4 copy-done
  203.0 1.7 copy.77
  204.7 8.7 %all-to-all-start.2 = ((bf16[64,64,128]{2,1,0:T(8,128)(2,1)}), bf16[64,64,128]{2,1,0:T(8,128)(2,1)S(1)}, u32[]{:S(2)}, u32[]{:S(2)}) async-start(bf16[64,64,128]{2,1,0:T(8,128)(2,1)} %copy.77), calls=%async_computation.2 | async-start | bytes 2097152 | tf_op jit(solution)/shard_map/all_to_all | solution.py:127
  213.4 1.5 fusion.22
  215.6 1.2 fusion.29
  216.8 1.3 convolution_add_fusion
  218.1 1.4 copy-done.1
  219.8 1.6 copy.83
  221.5 15.4 %all-to-all-done.2 = bf16[64,64,128]{2,1,0:T(8,128)(2,1)S(1)} async-done(((bf16[64,64,128]{2,1,0:T(8,128)(2,1)}), bf16[64,64,128]{2,1,0:T(8,128)(2,1)S(1)}, u32[]{:S(2)}, u32[]{:S(2)}) %all-to-all-start.2) | async-done | bytes 1048608 | tf_op jit(solution)/shard_map/all_to_all | solution.py:127
  236.8 9.9 %all-to-all-start.4 = ((bf16[64,64,128]{2,1,0:T(8,128)(2,1)}), bf16[64,64,128]{2,1,0:T(8,128)(2,1)}, u32[]{:S(2)}, u32[]{:S(2)}) async-start(bf16[64,64,128]{2,1,0:T(8,128)(2,1)} %copy.83), calls=%async_computation.4 | async-start | bytes 2097152 | tf_op jit(solution)/shard_map/all_to_all | solution.py:134
  248.3 1.3 fusion.14
  249.8 1.3 fusion.12
  252.5 19.4 %all-to-all-done.4 = bf16[64,64,128]{2,1,0:T(8,128)(2,1)} async-done(((bf16[64,64,128]{2,1,0:T(8,128)(2,1)}), bf16[64,64,128]{2,1,0:T(8,128)(2,1)}, u32[]{:S(2)}, u32[]{:S(2)}) %all-to-all-start.4) | async-done | bytes 1048608 | tf_op jit(solution)/shard_map/all_to_all | solution.py:134
  271.9 2.0 fusion
  273.9 1.1 fusion.49
  275.8 9.5 %all-to-all-start.3 = ((bf16[2,64,128]{2,0,1:T(2,128)(2,1)}), bf16[2,64,128]{2,0,1:T(2,128)(2,1)S(1)}, u32[]{:S(2)}, u32[]{:S(2)}) async-start(bf16[2,64,128]{2,0,1:T(2,128)(2,1)} %pad_maximum_fusion.2), calls=%async_computation.3 | async-start | bytes 65536 | tf_op jit(solution)/shard_map/all_to_all | solution.py:153
  285.2 1.1 fusion.47
  287.0 2.9 all-to-all-done.3
  289.9 4.0 %all-to-all-start.5 = ((bf16[2,64,128]{2,0,1:T(2,128)(2,1)}), bf16[2,64,128]{2,0,1:T(2,128)(2,1)S(1)}, u32[]{:S(2)}, u32[]{:S(2)}) async-start(bf16[2,64,128]{2,0,1:T(2,128)(2,1)} %pad_maximum_fusion.3), calls=%async_computation.5 | async-start | bytes 65536 | tf_op jit(solution)/shard_map/all_to_all | solution.py:154
  295.2 3.4 %all-to-all-done.5 = bf16[2,64,128]{2,0,1:T(2,128)(2,1)S(1)} async-done(((bf16[2,64,128]{2,0,1:T(2,128)(2,1)}), bf16[2,64,128]{2,0,1:T(2,128)(2,1)S(1)}, u32[]{:S(2)}, u32[]{:S(2)}) %all-to-all-start.5) | async-done | bytes 32800 | tf_op jit(solution)/shard_map/all_to_all | solution.py:154
  (126 shorter events, 19.1 us)
Async XLA Ops:
  7.2 17.3 %copy-start.14 = (bf16[2,8,1024]{2,1,0:T(8,128)(2,1)S(1)}, bf16[2,8,1024]{2,1,0:T(8,128)(2,1)}, u32[]{:S(2)}) copy-start(bf16[2,8,1024]{2,1,0:T(8,128)(2,1)} %param.8) | copy-start | bytes 98308
  7.2 27.7 %copy-start.26 = (s32[128]{0:T(128)S(1)}, s32[128]{0:T(128)}, u32[]{:S(2)}) copy-start(s32[128]{0:T(128)} %param.11) | copy-start | bytes 1540
  7.2 28.1 %copy-start.15 = (s32[4,128,8]{1,2,0:T(8,128)S(1)}, s32[4,128,8]{1,2,0:T(8,128)}, u32[]{:S(2)}) copy-start(s32[4,128,8]{1,2,0:T(8,128)} %param.10) | copy-start | bytes 49156
  7.2 29.3 %copy-start.5 = (bf16[2,64,1024]{2,1,0:T(8,128)(2,1)S(1)}, bf16[2,64,1024]{2,1,0:T(8,128)(2,1)}, u32[]{:S(2)}) copy-start(bf16[2,64,1024]{2,1,0:T(8,128)(2,1)} %param.6) | copy-start | bytes 786436
  7.2 95.8 %all-gather.5.cloned.1.call-start = ((), (), s32[]{:S(2)}) async-start(), calls=%async_computation.7 | async-start | bytes 2129920 | tf_op jit(solution)/shard_map/all_gather | solution.py:92
  22.8 13.8 %copy-start.6 = (bf16[2,64,1024]{2,1,0:T(8,128)(2,1)S(1)}, bf16[2,64,1024]{2,1,0:T(8,128)(2,1)}, u32[]{:S(2)}) copy-start(bf16[2,64,1024]{2,1,0:T(8,128)(2,1)} %param.9) | copy-start | bytes 786436
  24.4 162.5 %all-gather.3.cloned.1.call-start = ((), (), s32[]{:S(2)}) async-start(), calls=%async_computation.6 | async-start | bytes 2129920 | tf_op jit(solution)/shard_map/all_gather | solution.py:93
  36.0 162.8 %copy-start.20 = (pred[8]{0:T(512)(128)(4,1)}, pred[8]{0:T(512)(128)(4,1)S(1)}, u32[]{:S(2)}) copy-start(pred[8]{0:T(512)(128)(4,1)S(1)} %not.36) | copy-start | bytes 28
  36.0 164.0 %copy-start.22 = (pred[8]{0:T(512)(128)(4,1)}, pred[8]{0:T(512)(128)(4,1)S(1)}, u32[]{:S(2)}) copy-start(pred[8]{0:T(512)(128)(4,1)S(1)} %not.38) | copy-start | bytes 28
  36.7 160.3 %copy-start.8 = (bf16[8,8,8,128]{3,2,1,0:T(8,128)(2,1)}, bf16[8,8,8,128]{3,2,1,0:T(8,128)(2,1)S(1)}, u32[]{:S(2)}) copy-start(bf16[8,8,8,128]{3,2,1,0:T(8,128)(2,1)S(1)} %copy.87) | copy-start | bytes 393220
  36.7 152.7 %copy-start.10 = (bf16[8,8,8,128]{3,2,1,0:T(8,128)(2,1)}, bf16[8,8,8,128]{3,2,1,0:T(8,128)(2,1)S(1)}, u32[]{:S(2)}) copy-start(bf16[8,8,8,128]{3,2,1,0:T(8,128)(2,1)S(1)} %copy.88) | copy-start | bytes 393220
  36.8 162.0 %copy-start.16 = (s32[8]{0:T(128)}, s32[8]{0:T(128)S(1)}, u32[]{:S(2)}) copy-start(s32[8]{0:T(128)S(1)} %get-tuple-element.21) | copy-start | bytes 100
  36.8 163.2 %copy-start.18 = (s32[8]{0:T(128)}, s32[8]{0:T(128)S(1)}, u32[]{:S(2)}) copy-start(s32[8]{0:T(128)S(1)} %get-tuple-element.20) | copy-start | bytes 100
  189.1 0.7 copy-start.11
  190.1 0.8 copy-start.2
  198.0 0.8 copy-start.3
  198.0 2.0 copy-start.7
  201.3 1.4 copy-start
  204.7 32.1 %all-to-all-start.2 = ((bf16[64,64,128]{2,1,0:T(8,128)(2,1)}), bf16[64,64,128]{2,1,0:T(8,128)(2,1)S(1)}, u32[]{:S(2)}, u32[]{:S(2)}) async-start(bf16[64,64,128]{2,1,0:T(8,128)(2,1)} %copy.77), calls=%async_computation.2 | async-start | bytes 2097152 | tf_op jit(solution)/shard_map/all_to_all | solution.py:127
  213.4 1.5 copy-start.9
  214.9 0.7 copy-start.17
  214.9 0.7 copy-start.21
  215.5 1.3 copy-start.19
  215.5 1.3 copy-start.23
  218.1 1.4 copy-start.1
  219.8 27.9 %copy-start.12 = (bf16[8,64,128]{2,1,0:T(8,128)(2,1)S(1)}, bf16[8,64,128]{2,1,0:T(8,128)(2,1)}, u32[]{:S(2)}) copy-start(bf16[8,64,128]{2,1,0:T(8,128)(2,1)} %copy-done.11) | copy-start | bytes 393220
  236.8 35.1 %all-to-all-start.4 = ((bf16[64,64,128]{2,1,0:T(8,128)(2,1)}), bf16[64,64,128]{2,1,0:T(8,128)(2,1)}, u32[]{:S(2)}, u32[]{:S(2)}) async-start(bf16[64,64,128]{2,1,0:T(8,128)(2,1)} %copy.83), calls=%async_computation.4 | async-start | bytes 2097152 | tf_op jit(solution)/shard_map/all_to_all | solution.py:134
  249.8 1.5 copy-start.4
  249.8 22.1 %copy-start.24 = (f32[64]{0:T(128)S(1)}, f32[64]{0:T(128)}, u32[]{:S(2)}) copy-start(f32[64]{0:T(128)} %broadcast_subtract_fusion) | copy-start | bytes 772
  249.8 22.1 %copy-start.25 = (f32[64]{0:T(128)S(1)}, f32[64]{0:T(128)}, u32[]{:S(2)}) copy-start(f32[64]{0:T(128)} %compare_convert_fusion) | copy-start | bytes 772
  275.8 14.2 %all-to-all-start.3 = ((bf16[2,64,128]{2,0,1:T(2,128)(2,1)}), bf16[2,64,128]{2,0,1:T(2,128)(2,1)S(1)}, u32[]{:S(2)}, u32[]{:S(2)}) async-start(bf16[2,64,128]{2,0,1:T(2,128)(2,1)} %pad_maximum_fusion.2), calls=%async_computation.3 | async-start | bytes 65536 | tf_op jit(solution)/shard_map/all_to_all | solution.py:153
  289.9 8.7 %all-to-all-start.5 = ((bf16[2,64,128]{2,0,1:T(2,128)(2,1)}), bf16[2,64,128]{2,0,1:T(2,128)(2,1)S(1)}, u32[]{:S(2)}, u32[]{:S(2)}) async-start(bf16[2,64,128]{2,0,1:T(2,128)(2,1)} %pad_maximum_fusion.3), calls=%async_computation.5 | async-start | bytes 65536 | tf_op jit(solution)/shard_map/all_to_all | solution.py:154
  (1 other events, 0.7 us)
Sparse Core Ops, SparseCore 0:
  24.5 78.4 all-gather.4
  106.6 80.2 all-gather.2
where the time goes:
time: 307 us; the launch traced here: 306 us
  waiting for transfers between devices  188 us (61%)
  starting transfers between devices  32.1 us (10%)
  local copies, waits for them, and re-layouts  25.6 us (8%)
  blocking collectives  21.7 us (7%)
  between operations  14.8 us (5%)
  matrix products  13.3 us (4%)
  other arithmetic  10.4 us (3%)
    all_gather x1, waiting for transfers between devices, body(): lax.all_gather(mine_values, 'seq', axis=0, tiled=True)  81 us
    all_gather x1, waiting for transfers between devices, body(): lax.all_gather(mine_keys, 'seq', axis=0, tiled=True)  66.1 us
    all_to_all x1, waiting for transfers between devices, body(): lax.all_to_all(value_buffer[:seq_count].astype(jnp.bfloat16), 'seq', spli...  19.4 us
    all_to_all x1, waiting for transfers between devices, body(): lax.all_to_all(key_buffer[:seq_count].astype(jnp.bfloat16), 'seq', split_...  15.4 us
    all_to_all x1, blocking collectives, body(): lax.all_to_all(key_states, 'head', split_axis=2, concat_axis=1, tiled=True)  13.9 us
    all_to_all x1, starting transfers between devices, body(): lax.all_to_all(value_buffer[:seq_count].astype(jnp.bfloat16), 'seq', spli...  9.89 us
    all_to_all x1, starting transfers between devices, body(): lax.all_to_all(key_total, 'head', split_axis=1, concat_axis=2, tiled=True)  9.46 us
    all_to_all x1, starting transfers between devices, body(): lax.all_to_all(key_buffer[:seq_count].astype(jnp.bfloat16), 'seq', split_...  8.74 us
  transfers between devices with their start and end apart: 6, of which 6 were waited for; matrix products, arithmetic and copies ran while one was open for 7% of the time, Pallas kernels for 0%

commit v1 on v0

--- a/solution.py
+++ b/solution.py
@@ -77,7 +77,12 @@
     halfway = count_of_blocks // 2
     mine_keys, mine_values = (
         lax.all_to_all(key_states, "head", split_axis=2, concat_axis=1, tiled=True),
-        lax.all_to_all(value_state_rows, "head", split_axis=2, concat_axis=1, tiled=True),
+        jnp.concatenate(
+            lax.all_to_all(
+                jnp.stack(jnp.split(value_state_rows, lax.axis_size("head"), axis=2)), "head", 0, 0
+            ),
+            axis=1,
+        ),
     )
     qblocks = jnp.stack([device, count_of_blocks - 1 - device])
     pick_block = jnp.arange(count_of_blocks, dtype=jnp.int32)[None, :] == qblocks[:, None]

time: 307 us -> 307 us (level)
    unnamed x66 -> x70, local copies, waits for them, and re-layouts: 8.57 us -> 9.19 us
where the time goes in v1:
time: 307 us; the launch traced here: 306 us
  waiting for transfers between devices  188 us (61%)
  starting transfers between devices  32.1 us (10%)
  local copies, waits for them, and re-layouts  25.9 us (8%)
  blocking collectives  21.7 us (7%)
  between operations  14.7 us (5%)
  matrix products  13.2 us (4%)
  other arithmetic  10.4 us (3%)
    all_gather x1, waiting for transfers between devices, body(): lax.all_gather(mine_values, 'seq', axis=0, tiled=True)  81 us
    all_gather x1, waiting for transfers between devices, body(): lax.all_gather(mine_keys, 'seq', axis=0, tiled=True)  65.8 us
    all_to_all x1, waiting for transfers between devices, body(): lax.all_to_all(value_buffer[:seq_count].astype(jnp.bfloat16), 'seq', spli...  19.4 us
    all_to_all x1, waiting for transfers between devices, body(): lax.all_to_all(key_buffer[:seq_count].astype(jnp.bfloat16), 'seq', split_...  15.4 us
    all_to_all x1, blocking collectives, body(): lax.all_to_all(key_states, 'head', split_axis=2, concat_axis=1, tiled=True)  13.9 us
    all_to_all x1, starting transfers between devices, body(): lax.all_to_all(value_buffer[:seq_count].astype(jnp.bfloat16), 'seq', spli...  9.89 us
    all_to_all x1, starting transfers between devices, body(): lax.all_to_all(key_total, 'head', split_axis=1, concat_axis=2, tiled=True)  9.46 us
    unnamed x70, local copies, waits for them, and re-layouts  9.19 us
  transfers between devices with their start and end apart: 6, of which 6 were waited for; matrix products, arithmetic and copies ran while one was open for 7% of the time, Pallas kernels for 0%

profile of v1, /device:TPU:1, one launch (start us, length us, event | category | flops | bytes accessed | tf_op | source)
XLA Modules:
  0.0 306.1 jit_solution(2717361965055213140)
XLA Ops:
  7.3 1.1 copy.61
  8.9 13.9 %all_to_all.69 = bf16[8,2,1024]{2,1,0:T(2,128)(2,1)S(1)} all-to-all(bf16[8,2,1024]{2,1,0:T(2,128)(2,1)S(1)} %reshape.435), channel_id=1, replica_groups=mesh['seq'=64,'head'=8] {'head'}, dimensions={0} | all-to-all | bytes 65536 | tf_op jit(solution)/shard_map/all_to_all | solution.py:79
  26.6 7.8 %all_to_all.70 = bf16[8,2,8,128]{3,2,1,0:T(8,128)(2,1)S(1)} all-to-all(bf16[8,2,8,128]{3,2,1,0:T(8,128)(2,1)S(1)} %constant_dynamic-update-slice_fusion), channel_id=1, replica_groups=mesh['seq'=64,'head'=8] {'head'}, dimensions={0} | all-to-all | bytes 65536 | tf_op jit(solution)/shard_map/all_to_all | solution.py:81
  37.2 65.8 %all-gather.5.cloned.1.call-done = bf16[128,64,128]{2,1,0:T(8,128)(2,1)} async-done(((bf16[2,64,128]{2,1,0:T(8,128)(2,1)}), bf16[128,64,128]{2,1,0:T(8,128)(2,1)}) %all-gather.5.cloned.1.call-update) | async-done | bytes 2097168 | tf_op jit(solution)/shard_map/all_gather | solution.py:97
  103.0 2.2 gather_fusion.3
  105.9 81.0 %all-gather.3.cloned.1.call-done = bf16[128,64,128]{2,1,0:T(8,128)(2,1)} async-done(((bf16[2,64,128]{2,1,0:T(8,128)(2,1)}), bf16[128,64,128]{2,1,0:T(8,128)(2,1)}) %all-gather.3.cloned.1.call-update) | async-done | bytes 2097168 | tf_op jit(solution)/shard_map/all_gather | solution.py:98
  186.9 2.2 gather_fusion.2
  190.9 1.0 fusion.8
  191.9 2.2 gather_fusion.1
  194.8 2.2 gather_fusion
  198.8 1.2 fusion.32
  200.0 1.3 convolution_add_fusion.1
  201.3 1.4 copy-done
  203.0 1.7 copy.75
  204.7 8.7 %all-to-all-start.2 = ((bf16[64,64,128]{2,1,0:T(8,128)(2,1)}), bf16[64,64,128]{2,1,0:T(8,128)(2,1)S(1)}, u32[]{:S(2)}, u32[]{:S(2)}) async-start(bf16[64,64,128]{2,1,0:T(8,128)(2,1)} %copy.75), calls=%async_computation.2 | async-start | bytes 2097152 | tf_op jit(solution)/shard_map/all_to_all | solution.py:132
  213.5 1.5 fusion.22
  215.6 1.2 fusion.29
  216.8 1.3 convolution_add_fusion
  218.1 1.4 copy-done.1
  219.8 1.6 copy.81
  221.5 15.4 %all-to-all-done.2 = bf16[64,64,128]{2,1,0:T(8,128)(2,1)S(1)} async-done(((bf16[64,64,128]{2,1,0:T(8,128)(2,1)}), bf16[64,64,128]{2,1,0:T(8,128)(2,1)S(1)}, u32[]{:S(2)}, u32[]{:S(2)}) %all-to-all-start.2) | async-done | bytes 1048608 | tf_op jit(solution)/shard_map/all_to_all | solution.py:132
  236.8 9.9 %all-to-all-start.4 = ((bf16[64,64,128]{2,1,0:T(8,128)(2,1)}), bf16[64,64,128]{2,1,0:T(8,128)(2,1)}, u32[]{:S(2)}, u32[]{:S(2)}) async-start(bf16[64,64,128]{2,1,0:T(8,128)(2,1)} %copy.81), calls=%async_computation.4 | async-start | bytes 2097152 | tf_op jit(solution)/shard_map/all_to_all | solution.py:139
  248.3 1.3 fusion.14
  249.8 1.3 fusion.12
  252.6 19.4 %all-to-all-done.4 = bf16[64,64,128]{2,1,0:T(8,128)(2,1)} async-done(((bf16[64,64,128]{2,1,0:T(8,128)(2,1)}), bf16[64,64,128]{2,1,0:T(8,128)(2,1)}, u32[]{:S(2)}, u32[]{:S(2)}) %all-to-all-start.4) | async-done | bytes 1048608 | tf_op jit(solution)/shard_map/all_to_all | solution.py:139
  271.9 2.0 fusion
  274.0 1.1 fusion.49
  275.8 9.5 %all-to-all-start.3 = ((bf16[2,64,128]{2,0,1:T(2,128)(2,1)}), bf16[2,64,128]{2,0,1:T(2,128)(2,1)S(1)}, u32[]{:S(2)}, u32[]{:S(2)}) async-start(bf16[2,64,128]{2,0,1:T(2,128)(2,1)} %pad_maximum_fusion.2), calls=%async_computation.3 | async-start | bytes 65536 | tf_op jit(solution)/shard_map/all_to_all | solution.py:158
  285.2 1.1 fusion.47
  287.0 2.9 all-to-all-done.3
  290.0 4.0 %all-to-all-start.5 = ((bf16[2,64,128]{2,0,1:T(2,128)(2,1)}), bf16[2,64,128]{2,0,1:T(2,128)(2,1)S(1)}, u32[]{:S(2)}, u32[]{:S(2)}) async-start(bf16[2,64,128]{2,0,1:T(2,128)(2,1)} %pad_maximum_fusion.3), calls=%async_computation.5 | async-start | bytes 65536 | tf_op jit(solution)/shard_map/all_to_all | solution.py:159
  295.3 3.4 %all-to-all-done.5 = bf16[2,64,128]{2,0,1:T(2,128)(2,1)S(1)} async-done(((bf16[2,64,128]{2,0,1:T(2,128)(2,1)}), bf16[2,64,128]{2,0,1:T(2,128)(2,1)S(1)}, u32[]{:S(2)}, u32[]{:S(2)}) %all-to-all-start.5) | async-done | bytes 32800 | tf_op jit(solution)/shard_map/all_to_all | solution.py:159
  (131 shorter events, 19.4 us)
Async XLA Ops:
  7.2 19.4 %copy-start.14 = (bf16[2,8,1024]{2,1,0:T(8,128)(2,1)S(1)}, bf16[2,8,1024]{2,1,0:T(8,128)(2,1)}, u32[]{:S(2)}) copy-start(bf16[2,8,1024]{2,1,0:T(8,128)(2,1)} %param.8) | copy-start | bytes 98308
  7.2 28.0 %copy-start.26 = (s32[128]{0:T(128)S(1)}, s32[128]{0:T(128)}, u32[]{:S(2)}) copy-start(s32[128]{0:T(128)} %param.11) | copy-start | bytes 1540
  7.2 28.4 %copy-start.15 = (s32[4,128,8]{1,2,0:T(8,128)S(1)}, s32[4,128,8]{1,2,0:T(8,128)}, u32[]{:S(2)}) copy-start(s32[4,128,8]{1,2,0:T(8,128)} %param.10) | copy-start | bytes 49156
  7.2 29.7 %copy-start.5 = (bf16[2,64,1024]{2,1,0:T(8,128)(2,1)S(1)}, bf16[2,64,1024]{2,1,0:T(8,128)(2,1)}, u32[]{:S(2)}) copy-start(bf16[2,64,1024]{2,1,0:T(8,128)(2,1)} %param.6) | copy-start | bytes 786436
  7.2 29.7 %copy-start.6 = (bf16[2,64,1024]{2,1,0:T(8,128)(2,1)S(1)}, bf16[2,64,1024]{2,1,0:T(8,128)(2,1)}, u32[]{:S(2)}) copy-start(bf16[2,64,1024]{2,1,0:T(8,128)(2,1)} %param.9) | copy-start | bytes 786436
  7.2 95.8 %all-gather.5.cloned.1.call-start = ((), (), s32[]{:S(2)}) async-start(), calls=%async_computation.7 | async-start | bytes 2129920 | tf_op jit(solution)/shard_map/all_gather | solution.py:97
  24.4 162.5 %all-gather.3.cloned.1.call-start = ((), (), s32[]{:S(2)}) async-start(), calls=%async_computation.6 | async-start | bytes 2129920 | tf_op jit(solution)/shard_map/all_gather | solution.py:98
  36.3 162.5 %copy-start.20 = (pred[8]{0:T(512)(128)(4,1)}, pred[8]{0:T(512)(128)(4,1)S(1)}, u32[]{:S(2)}) copy-start(pred[8]{0:T(512)(128)(4,1)S(1)} %not.36) | copy-start | bytes 28
  36.3 163.7 %copy-start.22 = (pred[8]{0:T(512)(128)(4,1)}, pred[8]{0:T(512)(128)(4,1)S(1)}, u32[]{:S(2)}) copy-start(pred[8]{0:T(512)(128)(4,1)S(1)} %not.38) | copy-start | bytes 28
  37.0 160.0 %copy-start.8 = (bf16[8,8,8,128]{3,2,1,0:T(8,128)(2,1)}, bf16[8,8,8,128]{3,2,1,0:T(8,128)(2,1)S(1)}, u32[]{:S(2)}) copy-start(bf16[8,8,8,128]{3,2,1,0:T(8,128)(2,1)S(1)} %copy.85) | copy-start | bytes 393220
  37.0 152.5 %copy-start.10 = (bf16[8,8,8,128]{3,2,1,0:T(8,128)(2,1)}, bf16[8,8,8,128]{3,2,1,0:T(8,128)(2,1)S(1)}, u32[]{:S(2)}) copy-start(bf16[8,8,8,128]{3,2,1,0:T(8,128)(2,1)S(1)} %copy.86) | copy-start | bytes 393220
  37.1 161.7 %copy-start.16 = (s32[8]{0:T(128)}, s32[8]{0:T(128)S(1)}, u32[]{:S(2)}) copy-start(s32[8]{0:T(128)S(1)} %get-tuple-element.21) | copy-start | bytes 100
  37.1 162.9 %copy-start.18 = (s32[8]{0:T(128)}, s32[8]{0:T(128)S(1)}, u32[]{:S(2)}) copy-start(s32[8]{0:T(128)S(1)} %get-tuple-element.20) | copy-start | bytes 100
  189.1 0.7 copy-start.11
  190.1 0.8 copy-start.2
  198.0 0.8 copy-start.3
  198.0 2.0 copy-start.7
  201.3 1.4 copy-start
  204.7 32.1 %all-to-all-start.2 = ((bf16[64,64,128]{2,1,0:T(8,128)(2,1)}), bf16[64,64,128]{2,1,0:T(8,128)(2,1)S(1)}, u32[]{:S(2)}, u32[]{:S(2)}) async-start(bf16[64,64,128]{2,1,0:T(8,128)(2,1)} %copy.75), calls=%async_computation.2 | async-start | bytes 2097152 | tf_op jit(solution)/shard_map/all_to_all | solution.py:132
  213.5 1.5 copy-start.9
  215.0 0.7 copy-start.17
  215.0 0.7 copy-start.21
  215.5 1.3 copy-start.19
  215.5 1.3 copy-start.23
  218.1 1.4 copy-start.1
  219.8 27.9 %copy-start.12 = (bf16[8,64,128]{2,1,0:T(8,128)(2,1)S(1)}, bf16[8,64,128]{2,1,0:T(8,128)(2,1)}, u32[]{:S(2)}) copy-start(bf16[8,64,128]{2,1,0:T(8,128)(2,1)} %copy-done.11) | copy-start | bytes 393220
  236.8 35.1 %all-to-all-start.4 = ((bf16[64,64,128]{2,1,0:T(8,128)(2,1)}), bf16[64,64,128]{2,1,0:T(8,128)(2,1)}, u32[]{:S(2)}, u32[]{:S(2)}) async-start(bf16[64,64,128]{2,1,0:T(8,128)(2,1)} %copy.81), calls=%async_computation.4 | async-start | bytes 2097152 | tf_op jit(solution)/shard_map/all_to_all | solution.py:139
  249.8 1.5 copy-start.4
  249.8 22.1 %copy-start.24 = (f32[64]{0:T(128)S(1)}, f32[64]{0:T(128)}, u32[]{:S(2)}) copy-start(f32[64]{0:T(128)} %broadcast_subtract_fusion) | copy-start | bytes 772
  249.8 22.1 %copy-start.25 = (f32[64]{0:T(128)S(1)}, f32[64]{0:T(128)}, u32[]{:S(2)}) copy-start(f32[64]{0:T(128)} %compare_convert_fusion) | copy-start | bytes 772
  275.8 14.2 %all-to-all-start.3 = ((bf16[2,64,128]{2,0,1:T(2,128)(2,1)}), bf16[2,64,128]{2,0,1:T(2,128)(2,1)S(1)}, u32[]{:S(2)}, u32[]{:S(2)}) async-start(bf16[2,64,128]{2,0,1:T(2,128)(2,1)} %pad_maximum_fusion.2), calls=%async_computation.3 | async-start | bytes 65536 | tf_op jit(solution)/shard_map/all_to_all | solution.py:158
  290.0 8.7 %all-to-all-start.5 = ((bf16[2,64,128]{2,0,1:T(2,128)(2,1)}), bf16[2,64,128]{2,0,1:T(2,128)(2,1)S(1)}, u32[]{:S(2)}, u32[]{:S(2)}) async-start(bf16[2,64,128]{2,0,1:T(2,128)(2,1)} %pad_maximum_fusion.3), calls=%async_computation.5 | async-start | bytes 65536 | tf_op jit(solution)/shard_map/all_to_all | solution.py:159
  (1 other events, 0.7 us)
Sparse Core Ops, SparseCore 0:
  24.5 78.4 all-gather.4
  106.6 80.2 all-gather.2
